TPU v7x, 512 devices: a whole 4x8x8 slice. The times are simulated.
512 devices in a mesh: ctx: 32 (over y_lo, z, core), tp: 16 (over x, y_hi).
Axes of the slice: x: 4, y: 8 (y_hi: 4, y_lo: 2; y = y_hi * 2 + y_lo), z: 8, core: 2. Of those that a mesh axis runs over, the one named last changes fastest.
Arguments:
- query: bfloat16 [8192, 4096], P('ctx', 'tp'), may hold values from 0.049804688 to 2
- key_feat: bfloat16 [8192, 4096], P('ctx', 'tp'), may hold values from 0.049804688 to 2
- value: bfloat16 [8192, 4096], P('ctx', 'tp'), may hold values from -36 to 36
- grad_out: bfloat16 [8192, 4096], P('ctx', 'tp'), may hold values from -6 to 6
- w_out: bfloat16 [4096, 4096], P('tp', 'ctx'), may hold values from -0.09375 to 0.09375
Outputs:
- grad_query: bfloat16 [8192, 4096], P('ctx', 'tp')
- grad_key: bfloat16 [8192, 4096], P('ctx', 'tp')
- grad_value: bfloat16 [8192, 4096], P('ctx', 'tp')
All inputs are finite; a program needn't handle non-finite values.
Results may differ from a plain program's by a relative error of at most 0.0059.
Values may be sent and summed in bfloat16 or wider, within the bound.
No kernel may reach another device: no remote copies, remote signals or barrier semaphores. Data moves between devices by JAX's collectives and lax.ppermute only.
A program may use at most 64 MiB of HBM per device.

v0:
```python
import jax
import jax.numpy as jnp
from jax import lax
from jax.sharding import Mesh
from jax.sharding import PartitionSpec as P

E = 128
epsilon = 1e-06
highest = lax.Precision.HIGHEST
CTX = ("ylo", "z", "core")
TP = ("x", "yhi")
CHIPS = ("ylo", "z")


def swap_cores(value):
    return lax.ppermute(value, "core", [(0, 1), (1, 0)])


def ctx_scan(local_state, backward):
    core = lax.axis_index("core")
    other = swap_cores(local_state)
    first = jnp.where(core == 0, local_state, other)
    second = jnp.where(core == 0, other, local_state)
    chip_total = first + second
    if backward:
        within = jnp.where(core == 0, other, jnp.zeros_like(other))
    else:
        within = jnp.where(core == 1, other, jnp.zeros_like(other))
    half = lax.dynamic_index_in_dim(chip_total, core, 0, keepdims=False)
    chips = lax.axis_size("ylo") * lax.axis_size("z")
    window = half
    below = jnp.zeros_like(half)
    distance = 1
    while distance < chips:
        if backward:
            pairs = [(q, q - distance) for q in range(distance, chips)]
        else:
            pairs = [(q, q + distance) for q in range(chips - distance)]
        arrived = lax.ppermute(window, CHIPS, pairs)
        below = below + arrived
        if distance * 2 < chips:
            window = window + arrived
        distance *= 2
    other_half = swap_cores(below)
    head0 = jnp.where(core == 0, below, other_half)
    head1 = jnp.where(core == 0, other_half, below)
    return jnp.stack([head0, head1]) + within


def local(query, key_feat, value, grad_out, w_out):
    tok_rows = query.shape[0]
    feat_width = query.shape[1]
    head_count = feat_width // E
    full_rows = lax.all_gather(grad_out, TP, axis=1, tiled=True)
    grad_z = lax.dot_general(
        full_rows,
        lax.all_gather(w_out, CTX, axis=1, tiled=True),
        (((1,), (1,)), ((), ())),
        preferred_element_type=jnp.float32,
    )
    query_heads = query.reshape(tok_rows, head_count, E)
    key_heads = key_feat.reshape(tok_rows, head_count, E)
    value_heads = value.reshape(tok_rows, head_count, E)
    gradz_heads = grad_z.reshape(tok_rows, head_count, E)
    query_wide = query_heads.astype(jnp.float32)
    key_wide = key_heads.astype(jnp.float32)
    value_wide = value_heads.astype(jnp.float32)
    causal = (
        lax.broadcasted_iota(jnp.int32, (tok_rows, tok_rows), 0)
        >= lax.broadcasted_iota(jnp.int32, (tok_rows, tok_rows), 1)
    )[None]
    scores = jnp.einsum("thd,shd->hts", query_heads, key_heads, preferred_element_type=jnp.float32)
    weights = jnp.where(causal, scores, 0.0)
    local_state = jnp.einsum(
        "shd,she->hde", key_heads, value_heads, preferred_element_type=jnp.float32
    )
    state_in = ctx_scan(local_state, False)
    attended = jnp.einsum("hts,she->the", weights, value_wide, precision=highest)
    attended = attended + jnp.einsum("thd,hde->the", query_wide, state_in, precision=highest)
    inv_rms = lax.rsqrt(jnp.mean(attended * attended, axis=-1, keepdims=True) + epsilon)
    normed = attended * inv_rms
    grad_att = (
        inv_rms * (gradz_heads - normed * jnp.mean(gradz_heads * normed, axis=-1, keepdims=True))
    ).astype(jnp.bfloat16)
    grad_wide = grad_att.astype(jnp.float32)
    grad_weights = jnp.where(
        causal,
        jnp.einsum("the,she->hts", grad_att, value_heads, preferred_element_type=jnp.float32),
        0.0,
    )
    grad_query = jnp.einsum("hts,shd->thd", grad_weights, key_wide, precision=highest)
    grad_query = grad_query + jnp.einsum("the,hde->thd", grad_wide, state_in, precision=highest)
    local_adjoint = jnp.einsum(
        "thd,the->hde", query_heads, grad_att, preferred_element_type=jnp.float32
    )
    adjoint = ctx_scan(local_adjoint, True)
    grad_key = jnp.einsum("hts,thd->shd", grad_weights, query_wide, precision=highest)
    grad_key = grad_key + jnp.einsum("she,hde->shd", value_wide, adjoint, precision=highest)
    grad_value = jnp.einsum("hts,the->she", weights, grad_wide, precision=highest)
    grad_value = grad_value + jnp.einsum("shd,hde->she", key_wide, adjoint, precision=highest)
    return (
        grad_query.reshape(tok_rows, feat_width).astype(jnp.bfloat16),
        grad_key.reshape(tok_rows, feat_width).astype(jnp.bfloat16),
        grad_value.reshape(tok_rows, feat_width).astype(jnp.bfloat16),
    )


def solution(mesh):
    ctx_size, tp_size = mesh.devices.shape
    chips_y = 2
    fine = Mesh(
        mesh.devices.reshape(chips_y, ctx_size // (2 * chips_y), 2, tp_size // 4, 4), CTX + TP
    )
    return jax.shard_map(
        local,
        mesh=fine,
        in_specs=(P(CTX, TP), P(CTX, TP), P(CTX, TP), P(CTX, TP), P(TP, CTX)),
        out_specs=(P(CTX, TP), P(CTX, TP), P(CTX, TP)),
        check_vma=False,
    )
```

profile of v0, /device:TPU:3, one launch (start us, length us, event | category | flops | bytes accessed | tf_op | source)
XLA Modules:
  0.0 203.0 jit_solution(1962932447259268916)
XLA Ops:
  9.7 1.1 fusion.9
  10.8 2.6 %collective-permute-start = (f32[2,128,128]{2,1,0:T(8,128)S(1)}, f32[2,128,128]{2,1,0:T(8,128)S(1)}, u32[]{:S(2)}, u32[]{:S(2)}) collective-permute-start(f32[2,128,128]{2,1,0:T(8,128)S(1)} %fusion.9), channel_id=1, source_target_pairs={{0,16},{16,0},{1,17},{17,1},{2,18},{18,2},{3,19},{19,3},{4,20},{20... | collective-permute-start | bytes 393224 | tf_op jit(solution)/shard_map/ppermute | solution.py:16
  14.3 4.0 %collective-permute-start.1 = (f32[128,128]{1,0:T(8,128)S(1)}, f32[128,128]{1,0:T(8,128)S(1)}, u32[]{:S(2)}, u32[]{:S(2)}) collective-permute-start(f32[128,128]{1,0:T(8,128)S(1)} %add_bitcast_fusion.1), channel_id=1, source_target_pairs={{0,32},{32,64},{64,96},{96,128},{128,160},{160,192},{192,224},{224... | collective-permute-start | bytes 196616 | tf_op jit(solution)/shard_map/ppermute | solution.py:39
  18.3 1.3 collective-permute-done.1
  19.7 5.8 %collective-permute-start.2 = (f32[128,128]{1,0:T(8,128)S(1)}, f32[128,128]{1,0:T(8,128)S(1)}, u32[]{:S(2)}, u32[]{:S(2)}) collective-permute-start(f32[128,128]{1,0:T(8,128)S(1)} %add.79), channel_id=1, source_target_pairs={{0,64},{32,96},{64,128},{96,160},{128,192},{160,224},{192,256},{22... | collective-permute-start | bytes 196616 | tf_op jit(solution)/shard_map/ppermute | solution.py:39
  25.5 1.3 collective-permute-done.2
  26.8 12.1 %collective-permute-start.3 = (f32[128,128]{1,0:T(8,128)S(1)}, f32[128,128]{1,0:T(8,128)S(1)}, u32[]{:S(2)}, u32[]{:S(2)}) collective-permute-start(f32[128,128]{1,0:T(8,128)S(1)} %add.81), channel_id=1, source_target_pairs={{0,128},{32,160},{64,192},{96,224},{128,256},{160,288},{192,320},{... | collective-permute-start | bytes 196616 | tf_op jit(solution)/shard_map/ppermute | solution.py:39
  39.0 1.3 collective-permute-done.3
  40.3 8.7 %collective-permute-start.4 = (f32[128,128]{1,0:T(8,128)S(1)}, f32[128,128]{1,0:T(8,128)S(1)}, u32[]{:S(2)}, u32[]{:S(2)}) collective-permute-start(f32[128,128]{1,0:T(8,128)S(1)} %add.83), channel_id=1, source_target_pairs={{0,256},{32,288},{64,320},{96,352},{128,384},{160,416},{192,448},{... | collective-permute-start | bytes 196616 | tf_op jit(solution)/shard_map/ppermute | solution.py:39
  49.0 1.1 convolution_select_fusion.1
  50.3 5.7 %collective-permute-start.5 = (f32[128,128]{1,0:T(8,128)S(1)}, f32[128,128]{1,0:T(8,128)S(1)}, u32[]{:S(2)}, u32[]{:S(2)}) collective-permute-start(f32[128,128]{1,0:T(8,128)S(1)} %add_add_fusion.1), channel_id=1, source_target_pairs={{0,16},{16,0},{1,17},{17,1},{2,18},{18,2},{3,19},{19,3},{4,20},{20... | collective-permute-start | bytes 196616 | tf_op jit(solution)/shard_map/ppermute | solution.py:16
  57.3 21.5 %all-gather.3.cloned.1.call-done = bf16[256,4096]{1,0:T(8,128)(2,1)} async-done(((bf16[256,256]{1,0:T(8,128)(2,1)}), bf16[256,4096]{1,0:T(8,128)(2,1)}) %all-gather.3.cloned.1.call-update) | async-done | bytes 2097168 | tf_op jit(solution)/shard_map/all_gather | solution.py:54
  78.8 74.4 %all-gather.5.cloned.1.call-done = bf16[256,4096]{1,0:T(8,128)(2,1)} async-done(((bf16[256,128]{1,0:T(8,128)(2,1)}), bf16[256,4096]{1,0:T(8,128)(2,1)}) %all-gather.5.cloned.1.call-update) | async-done | bytes 2097168 | tf_op jit(solution)/shard_map/all_gather | solution.py:57
  153.3 3.0 %multiply_reduce_fusion = (f32[256,2]{0,1:T(2,128)S(1)}, f32[256,256]{0,1:T(8,128)S(1)}) fusion(f32[256,2,128]{0,2,1:T(8,128)S(1)} %get-tuple-element.11, f32[256,2]{0,1:T(2,128)S(1)} %add_rsqrt_fusion, bf16[256,4096]{1,0:T(8,128)(2,1)} %all-gather.3.cloned.1.call-done, bf16[256,4096]{1,0:T(8,128)(2,1)} %all-gather.5.cloned.1.call-done), kind=kOutput, calls=%fused_computation.17 | convolution fusion | flops 537067008 | bytes 4722688 | tf_op jit(solution)/shard_map/dot_general | solution.py:55
  156.5 2.2 %collective-permute-start.6 = (f32[2,128,128]{2,1,0:T(8,128)S(1)}, f32[2,128,128]{2,1,0:T(8,128)S(1)}, u32[]{:S(2)}, u32[]{:S(2)}) collective-permute-start(f32[2,128,128]{2,1,0:T(8,128)S(1)} %convolution_bitcast_fusion.6), channel_id=1, source_target_pairs={{0,16},{16,0},{1,17},{17,1},{2,18},{18,2},{3,19},{19,3},{4,20},{20... | collective-permute-start | bytes 393224 | tf_op jit(solution)/shard_map/ppermute | solution.py:16
  159.8 1.3 collective-permute-start.7
  161.4 3.4 %collective-permute-done.7 = f32[128,128]{1,0:T(8,128)S(1)} collective-permute-done((f32[128,128]{1,0:T(8,128)S(1)}, f32[128,128]{1,0:T(8,128)S(1)}, u32[]{:S(2)}, u32[]{:S(2)}) %collective-permute-start.7) | collective-permute-done | bytes 65568 | tf_op jit(solution)/shard_map/ppermute | solution.py:39
  164.8 1.3 collective-permute-start.8
  166.4 5.0 %collective-permute-done.8 = f32[128,128]{1,0:T(8,128)S(1)} collective-permute-done((f32[128,128]{1,0:T(8,128)S(1)}, f32[128,128]{1,0:T(8,128)S(1)}, u32[]{:S(2)}, u32[]{:S(2)}) %collective-permute-start.8) | collective-permute-done | bytes 65568 | tf_op jit(solution)/shard_map/ppermute | solution.py:39
  171.4 1.3 collective-permute-start.9
  173.2 7.2 %collective-permute-done.9 = f32[128,128]{1,0:T(8,128)S(1)} collective-permute-done((f32[128,128]{1,0:T(8,128)S(1)}, f32[128,128]{1,0:T(8,128)S(1)}, u32[]{:S(2)}, u32[]{:S(2)}) %collective-permute-start.9) | collective-permute-done | bytes 65568 | tf_op jit(solution)/shard_map/ppermute | solution.py:39
  180.4 1.3 collective-permute-start.10
  182.0 3.4 %collective-permute-done.10 = f32[128,128]{1,0:T(8,128)S(1)} collective-permute-done((f32[128,128]{1,0:T(8,128)S(1)}, f32[128,128]{1,0:T(8,128)S(1)}, u32[]{:S(2)}, u32[]{:S(2)}) %collective-permute-start.10) | collective-permute-done | bytes 65568 | tf_op jit(solution)/shard_map/ppermute | solution.py:39
  185.4 7.5 %collective-permute-start.11 = (f32[128,128]{1,0:T(8,128)S(1)}, f32[128,128]{1,0:T(8,128)S(1)}, u32[]{:S(2)}, u32[]{:S(2)}) collective-permute-start(f32[128,128]{1,0:T(8,128)S(1)} %add_add_fusion), channel_id=1, source_target_pairs={{0,16},{16,0},{1,17},{17,1},{2,18},{18,2},{3,19},{19,3},{4,20},{20... | collective-permute-start | bytes 196616 | tf_op jit(solution)/shard_map/ppermute | solution.py:16
  (45 shorter events, 10.8 us)
Async XLA Ops:
  7.2 41.8 %copy-start = (bf16[256,256]{1,0:T(8,128)(2,1)S(1)}, bf16[256,256]{1,0:T(8,128)(2,1)}, u32[]{:S(2)}) copy-start(bf16[256,256]{1,0:T(8,128)(2,1)} %param.5) | copy-start | bytes 393220
  7.2 48.9 %copy-start.1 = (bf16[256,256]{1,0:T(8,128)(2,1)S(1)}, bf16[256,256]{1,0:T(8,128)(2,1)}, u32[]{:S(2)}) copy-start(bf16[256,256]{1,0:T(8,128)(2,1)} %param.7) | copy-start | bytes 393220
  7.2 71.6 %all-gather.3.cloned.1.call-start = ((), (), s32[]{:S(2)}) async-start(), calls=%async_computation | async-start | bytes 2228224 | tf_op jit(solution)/shard_map/all_gather | solution.py:54
  7.9 145.3 %all-gather.5.cloned.1.call-start = ((), (), s32[]{:S(2)}) async-start(), calls=%async_computation.1 | async-start | bytes 2162688 | tf_op jit(solution)/shard_map/all_gather | solution.py:57
  10.8 3.6 %collective-permute-start = (f32[2,128,128]{2,1,0:T(8,128)S(1)}, f32[2,128,128]{2,1,0:T(8,128)S(1)}, u32[]{:S(2)}, u32[]{:S(2)}) collective-permute-start(f32[2,128,128]{2,1,0:T(8,128)S(1)} %fusion.9), channel_id=1, source_target_pairs={{0,16},{16,0},{1,17},{17,1},{2,18},{18,2},{3,19},{19,3},{4,20},{20... | collective-permute-start | bytes 393224 | tf_op jit(solution)/shard_map/ppermute | solution.py:16
  14.3 5.3 %collective-permute-start.1 = (f32[128,128]{1,0:T(8,128)S(1)}, f32[128,128]{1,0:T(8,128)S(1)}, u32[]{:S(2)}, u32[]{:S(2)}) collective-permute-start(f32[128,128]{1,0:T(8,128)S(1)} %add_bitcast_fusion.1), channel_id=1, source_target_pairs={{0,32},{32,64},{64,96},{96,128},{128,160},{160,192},{192,224},{224... | collective-permute-start | bytes 196616 | tf_op jit(solution)/shard_map/ppermute | solution.py:39
  19.7 7.1 %collective-permute-start.2 = (f32[128,128]{1,0:T(8,128)S(1)}, f32[128,128]{1,0:T(8,128)S(1)}, u32[]{:S(2)}, u32[]{:S(2)}) collective-permute-start(f32[128,128]{1,0:T(8,128)S(1)} %add.79), channel_id=1, source_target_pairs={{0,64},{32,96},{64,128},{96,160},{128,192},{160,224},{192,256},{22... | collective-permute-start | bytes 196616 | tf_op jit(solution)/shard_map/ppermute | solution.py:39
  26.8 13.5 %collective-permute-start.3 = (f32[128,128]{1,0:T(8,128)S(1)}, f32[128,128]{1,0:T(8,128)S(1)}, u32[]{:S(2)}, u32[]{:S(2)}) collective-permute-start(f32[128,128]{1,0:T(8,128)S(1)} %add.81), channel_id=1, source_target_pairs={{0,128},{32,160},{64,192},{96,224},{128,256},{160,288},{192,320},{... | collective-permute-start | bytes 196616 | tf_op jit(solution)/shard_map/ppermute | solution.py:39
  40.3 10.0 %collective-permute-start.4 = (f32[128,128]{1,0:T(8,128)S(1)}, f32[128,128]{1,0:T(8,128)S(1)}, u32[]{:S(2)}, u32[]{:S(2)}) collective-permute-start(f32[128,128]{1,0:T(8,128)S(1)} %add.83), channel_id=1, source_target_pairs={{0,256},{32,288},{64,320},{96,352},{128,384},{160,416},{192,448},{... | collective-permute-start | bytes 196616 | tf_op jit(solution)/shard_map/ppermute | solution.py:39
  50.3 6.6 %collective-permute-start.5 = (f32[128,128]{1,0:T(8,128)S(1)}, f32[128,128]{1,0:T(8,128)S(1)}, u32[]{:S(2)}, u32[]{:S(2)}) collective-permute-start(f32[128,128]{1,0:T(8,128)S(1)} %add_add_fusion.1), channel_id=1, source_target_pairs={{0,16},{16,0},{1,17},{17,1},{2,18},{18,2},{3,19},{19,3},{4,20},{20... | collective-permute-start | bytes 196616 | tf_op jit(solution)/shard_map/ppermute | solution.py:16
  156.5 3.2 %collective-permute-start.6 = (f32[2,128,128]{2,1,0:T(8,128)S(1)}, f32[2,128,128]{2,1,0:T(8,128)S(1)}, u32[]{:S(2)}, u32[]{:S(2)}) collective-permute-start(f32[2,128,128]{2,1,0:T(8,128)S(1)} %convolution_bitcast_fusion.6), channel_id=1, source_target_pairs={{0,16},{16,0},{1,17},{17,1},{2,18},{18,2},{3,19},{19,3},{4,20},{20... | collective-permute-start | bytes 393224 | tf_op jit(solution)/shard_map/ppermute | solution.py:16
  159.8 5.0 %collective-permute-start.7 = (f32[128,128]{1,0:T(8,128)S(1)}, f32[128,128]{1,0:T(8,128)S(1)}, u32[]{:S(2)}, u32[]{:S(2)}) collective-permute-start(f32[128,128]{1,0:T(8,128)S(1)} %add_bitcast_fusion), channel_id=1, source_target_pairs={{32,0},{64,32},{96,64},{128,96},{160,128},{192,160},{224,192},{256... | collective-permute-start | bytes 196616 | tf_op jit(solution)/shard_map/ppermute | solution.py:39
  164.8 6.6 %collective-permute-start.8 = (f32[128,128]{1,0:T(8,128)S(1)}, f32[128,128]{1,0:T(8,128)S(1)}, u32[]{:S(2)}, u32[]{:S(2)}) collective-permute-start(f32[128,128]{1,0:T(8,128)S(1)} %add.91), channel_id=1, source_target_pairs={{64,0},{96,32},{128,64},{160,96},{192,128},{224,160},{256,192},{28... | collective-permute-start | bytes 196616 | tf_op jit(solution)/shard_map/ppermute | solution.py:39
  166.4 27.6 %copy-start.2 = (bf16[256,256]{1,0:T(8,128)(2,1)S(1)}, bf16[256,256]{1,0:T(8,128)(2,1)}, u32[]{:S(2)}) copy-start(bf16[256,256]{1,0:T(8,128)(2,1)} %param.6) | copy-start | bytes 393220
  171.4 8.9 %collective-permute-start.9 = (f32[128,128]{1,0:T(8,128)S(1)}, f32[128,128]{1,0:T(8,128)S(1)}, u32[]{:S(2)}, u32[]{:S(2)}) collective-permute-start(f32[128,128]{1,0:T(8,128)S(1)} %add.93), channel_id=1, source_target_pairs={{128,0},{160,32},{192,64},{224,96},{256,128},{288,160},{320,192},{... | collective-permute-start | bytes 196616 | tf_op jit(solution)/shard_map/ppermute | solution.py:39
  180.4 5.0 %collective-permute-start.10 = (f32[128,128]{1,0:T(8,128)S(1)}, f32[128,128]{1,0:T(8,128)S(1)}, u32[]{:S(2)}, u32[]{:S(2)}) collective-permute-start(f32[128,128]{1,0:T(8,128)S(1)} %add.95), channel_id=1, source_target_pairs={{256,0},{288,32},{320,64},{352,96},{384,128},{416,160},{448,192},{... | collective-permute-start | bytes 196616 | tf_op jit(solution)/shard_map/ppermute | solution.py:39
  185.4 8.6 %collective-permute-start.11 = (f32[128,128]{1,0:T(8,128)S(1)}, f32[128,128]{1,0:T(8,128)S(1)}, u32[]{:S(2)}, u32[]{:S(2)}) collective-permute-start(f32[128,128]{1,0:T(8,128)S(1)} %add_add_fusion), channel_id=1, source_target_pairs={{0,16},{16,0},{1,17},{17,1},{2,18},{18,2},{3,19},{19,3},{4,20},{20... | collective-permute-start | bytes 196616 | tf_op jit(solution)/shard_map/ppermute | solution.py:16
Sparse Core Ops, SparseCore 0:
  11.0 67.7 all-gather.2
  80.9 72.3 all-gather.4
where the time goes:
time: 203 us
  waiting for transfers between devices  123 us (61%)
  starting transfers between devices  53.9 us (27%)
  between operations  14.3 us (7%)
  matrix products  8.44 us (4%)
  local copies, waits for them, and re-layouts  3.31 us (2%)
    all_gather x1, waiting for transfers between devices, local(): lax.all_gather(w_out, CTX, axis=1, tiled=True)  74.4 us
    ppermute x8, starting transfers between devices, ctx_scan(): arrived = lax.ppermute(window, CHIPS, pairs)  35.8 us
    ppermute x8, waiting for transfers between devices, ctx_scan(): arrived = lax.ppermute(window, CHIPS, pairs)  23 us
    all_gather x1, waiting for transfers between devices, local(): full_rows = lax.all_gather(grad_out, TP, axis=1, tiled=True)  21.5 us
    ppermute x4, starting transfers between devices, swap_cores(): return lax.ppermute(value, 'core', [(0, 1), (1, 0)])  18.1 us
  transfers between devices with their start and end apart: 14, of which 13 were waited for; matrix products, arithmetic and copies ran while one was open for 3% of the time, Pallas kernels for 0%

commit v1 on v0

--- a/solution.py
+++ b/solution.py
@@ -1,3 +1,4 @@
+import functools
 import jax
 import jax.numpy as jnp
 from jax import lax
@@ -10,6 +11,19 @@
 CTX = ("ylo", "z", "core")
 TP = ("x", "yhi")
 CHIPS = ("ylo", "z")
+
+
+def fix_the_lanes(sample, dim_no):
+    copies = []
+    for _ in range(lax.axis_size(CTX)):
+        copies.append(sample)
+    current_value = jnp.concatenate(
+        lax.all_to_all(jnp.stack(copies), axis_name=CTX, split_axis=0, concat_axis=0), axis=dim_no
+    )
+    return current_value
+
+
+copies_list = functools.partial(fix_the_lanes, dim_no=1)
 
 
 def swap_cores(value):
@@ -53,10 +67,7 @@
     head_count = feat_width // E
     full_rows = lax.all_gather(grad_out, TP, axis=1, tiled=True)
     grad_z = lax.dot_general(
-        full_rows,
-        lax.all_gather(w_out, CTX, axis=1, tiled=True),
-        (((1,), (1,)), ((), ())),
-        preferred_element_type=jnp.float32,
+        full_rows, copies_list(w_out), (((1,), (1,)), ((), ())), preferred_element_type=jnp.float32
     )
     query_heads = query.reshape(tok_rows, head_count, E)
     key_heads = key_feat.reshape(tok_rows, head_count, E)

time: 203 us -> 165 us (0.81)
  the two profiles are of different devices: /device:TPU:3 before, /device:TPU:17 now
where the time goes in v1:
time: 165 us; the launch traced here: 164 us
  waiting for transfers between devices  65.3 us (40%)
  starting transfers between devices  65.1 us (39%)
  between operations  14.4 us (9%)
  local copies, waits for them, and re-layouts  10.6 us (6%)
  matrix products  6.72 us (4%)
  other arithmetic  1.72 us (1%)
    ppermute x8, waiting for transfers between devices, ctx_scan(): arrived = lax.ppermute(window, CHIPS, pairs)  61.8 us
    ppermute x8, starting transfers between devices, ctx_scan(): arrived = lax.ppermute(window, CHIPS, pairs)  37.6 us
    ppermute x4, starting transfers between devices, swap_cores(): return lax.ppermute(value, 'core', [(0, 1), (1, 0)])  15.1 us
    all_to_all x1, starting transfers between devices, fix_the_lanes(): lax.all_to_all(jnp.stack(copies), axis_name=CTX, split_axis=0, concat_axi...  12.3 us
  transfers between devices with their start and end apart: 14, of which 11 were waited for; matrix products, arithmetic and copies ran while one was open for 7% of the time, Pallas kernels for 0%

profile of v1, /device:TPU:17, one launch (start us, length us, event | category | flops | bytes accessed | tf_op | source)
XLA Modules:
  0.0 163.9 jit_solution(16346426516387358921)
XLA Ops:
  7.2 2.7 %stack.17 = bf16[32,256,128]{2,1,0:T(8,128)(2,1)} broadcast(bf16[256,128]{1,0:T(8,128)(2,1)} %param.9), dimensions={1,2} | broadcast | bytes 2162688 | tf_op jit(solution)/shard_map/stack | solution.py:21
  9.8 12.3 %all-to-all-start = ((bf16[32,256,128]{2,1,0:T(8,128)(2,1)}), bf16[32,256,128]{2,1,0:T(8,128)(2,1)S(1)}, u32[]{:S(2)}, u32[]{:S(2)}) async-start(bf16[32,256,128]{2,1,0:T(8,128)(2,1)} %stack.17), calls=%async_computation | async-start | bytes 4194304 | tf_op jit(solution)/shard_map/all_to_all | solution.py:21
  23.2 2.1 %collective-permute-start = (f32[2,128,128]{2,1,0:T(8,128)S(1)}, f32[2,128,128]{2,1,0:T(8,128)S(1)}, u32[]{:S(2)}, u32[]{:S(2)}) collective-permute-start(f32[2,128,128]{2,1,0:T(8,128)S(1)} %fusion.11), channel_id=1, source_target_pairs={{0,16},{16,0},{1,17},{17,1},{2,18},{18,2},{3,19},{19,3},{4,20},{20... | collective-permute-start | bytes 393224 | tf_op jit(solution)/shard_map/ppermute | solution.py:30
  26.4 3.3 %collective-permute-start.1 = (f32[128,128]{1,0:T(8,128)S(1)}, f32[128,128]{1,0:T(8,128)S(1)}, u32[]{:S(2)}, u32[]{:S(2)}) collective-permute-start(f32[128,128]{1,0:T(8,128)S(1)} %add_bitcast_fusion.1), channel_id=1, source_target_pairs={{0,32},{32,64},{64,96},{96,128},{128,160},{160,192},{192,224},{224... | collective-permute-start | bytes 196616 | tf_op jit(solution)/shard_map/ppermute | solution.py:53
  29.7 39.2 %collective-permute-done.1 = f32[128,128]{1,0:T(8,128)S(1)} collective-permute-done((f32[128,128]{1,0:T(8,128)S(1)}, f32[128,128]{1,0:T(8,128)S(1)}, u32[]{:S(2)}, u32[]{:S(2)}) %collective-permute-start.1) | collective-permute-done | bytes 65568 | tf_op jit(solution)/shard_map/ppermute | solution.py:53
  69.0 6.0 %collective-permute-start.2 = (f32[128,128]{1,0:T(8,128)S(1)}, f32[128,128]{1,0:T(8,128)S(1)}, u32[]{:S(2)}, u32[]{:S(2)}) collective-permute-start(f32[128,128]{1,0:T(8,128)S(1)} %add.79), channel_id=1, source_target_pairs={{0,64},{32,96},{64,128},{96,160},{128,192},{160,224},{192,256},{22... | collective-permute-start | bytes 196616 | tf_op jit(solution)/shard_map/ppermute | solution.py:53
  74.9 1.3 collective-permute-done.2
  76.3 9.0 %collective-permute-start.3 = (f32[128,128]{1,0:T(8,128)S(1)}, f32[128,128]{1,0:T(8,128)S(1)}, u32[]{:S(2)}, u32[]{:S(2)}) collective-permute-start(f32[128,128]{1,0:T(8,128)S(1)} %add.81), channel_id=1, source_target_pairs={{0,128},{32,160},{64,192},{96,224},{128,256},{160,288},{192,320},{... | collective-permute-start | bytes 196616 | tf_op jit(solution)/shard_map/ppermute | solution.py:53
  85.3 1.3 collective-permute-done.3
  86.6 14.1 %collective-permute-start.4 = (f32[128,128]{1,0:T(8,128)S(1)}, f32[128,128]{1,0:T(8,128)S(1)}, u32[]{:S(2)}, u32[]{:S(2)}) collective-permute-start(f32[128,128]{1,0:T(8,128)S(1)} %add.83), channel_id=1, source_target_pairs={{0,256},{32,288},{64,320},{96,352},{128,384},{160,416},{192,448},{... | collective-permute-start | bytes 196616 | tf_op jit(solution)/shard_map/ppermute | solution.py:53
  102.7 3.4 %collective-permute-start.5 = (f32[128,128]{1,0:T(8,128)}, f32[128,128]{1,0:T(8,128)}, u32[]{:S(2)}, u32[]{:S(2)}) collective-permute-start(f32[128,128]{1,0:T(8,128)} %add_add_fusion.1), channel_id=1, source_target_pairs={{0,16},{16,0},{1,17},{17,1},{2,18},{18,2},{3,19},{19,3},{4,20},{20... | collective-permute-start | bytes 196616 | tf_op jit(solution)/shard_map/ppermute | solution.py:30
  109.3 2.7 %copy.35 = bf16[256,32,128]{2,1,0:T(8,128)(2,1)} copy(bf16[256,32,128]{2,0,1:T(8,128)(2,1)S(1)} %bitcast.117) | data formatting | bytes 4194304 | tf_op jit(solution)/shard_map/reshape | solution.py:20
  112.0 2.9 %dot_general.47 = bf16[2,128,4096]{2,1,0:T(8,128)(2,1)S(1)} reshape(bf16[256,32,128]{2,1,0:T(8,128)(2,1)} %copy.35) | data formatting | bytes 4194304 | tf_op jit(solution)/shard_map/dot_general | solution.py:69
  114.9 2.3 %multiply_reduce_fusion = (f32[256,2]{0,1:T(2,128)S(1)}, f32[256,2,128]{0,2,1:T(8,128)S(1)}) fusion(f32[256,2,128]{0,2,1:T(8,128)S(1)} %copy-done.3, f32[256,2]{0,1:T(2,128)S(1)} %add_rsqrt_fusion, bf16[2,128,4096]{2,1,0:T(8,128)(2,1)S(1)} %dot_general.47, bf16[256,4096]{1,0:T(8,128)(2,1)} %all-gather.2.cloned.1.call-done), kind=kOutput, calls=%fused_computation.19 | convolution fusion | flops 537067008 | bytes 4722688 | tf_op jit(solution)/shard_map/dot_general | solution.py:69
  117.5 2.3 %collective-permute-start.6 = (f32[2,128,128]{2,1,0:T(8,128)S(1)}, f32[2,128,128]{2,1,0:T(8,128)S(1)}, u32[]{:S(2)}, u32[]{:S(2)}) collective-permute-start(f32[2,128,128]{2,1,0:T(8,128)S(1)} %convolution_bitcast_fusion.6), channel_id=1, source_target_pairs={{0,16},{16,0},{1,17},{17,1},{2,18},{18,2},{3,19},{19,3},{4,20},{20... | collective-permute-start | bytes 393224 | tf_op jit(solution)/shard_map/ppermute | solution.py:30
  120.8 1.4 collective-permute-start.7
  122.6 3.4 %collective-permute-done.7 = f32[128,128]{1,0:T(8,128)S(1)} collective-permute-done((f32[128,128]{1,0:T(8,128)S(1)}, f32[128,128]{1,0:T(8,128)S(1)}, u32[]{:S(2)}, u32[]{:S(2)}) %collective-permute-start.7) | collective-permute-done | bytes 65568 | tf_op jit(solution)/shard_map/ppermute | solution.py:53
  126.0 1.3 collective-permute-start.8
  127.6 5.0 %collective-permute-done.8 = f32[128,128]{1,0:T(8,128)S(1)} collective-permute-done((f32[128,128]{1,0:T(8,128)S(1)}, f32[128,128]{1,0:T(8,128)S(1)}, u32[]{:S(2)}, u32[]{:S(2)}) %collective-permute-start.8) | collective-permute-done | bytes 65568 | tf_op jit(solution)/shard_map/ppermute | solution.py:53
  132.6 1.3 collective-permute-start.9
  134.2 7.3 %collective-permute-done.9 = f32[128,128]{1,0:T(8,128)S(1)} collective-permute-done((f32[128,128]{1,0:T(8,128)S(1)}, f32[128,128]{1,0:T(8,128)S(1)}, u32[]{:S(2)}, u32[]{:S(2)}) %collective-permute-start.9) | collective-permute-done | bytes 65568 | tf_op jit(solution)/shard_map/ppermute | solution.py:53
  141.5 1.3 collective-permute-start.10
  143.3 3.3 %collective-permute-done.10 = f32[128,128]{1,0:T(8,128)S(1)} collective-permute-done((f32[128,128]{1,0:T(8,128)S(1)}, f32[128,128]{1,0:T(8,128)S(1)}, u32[]{:S(2)}, u32[]{:S(2)}) %collective-permute-start.10) | collective-permute-done | bytes 65568 | tf_op jit(solution)/shard_map/ppermute | solution.py:53
  146.6 7.3 %collective-permute-start.11 = (f32[128,128]{1,0:T(8,128)S(1)}, f32[128,128]{1,0:T(8,128)S(1)}, u32[]{:S(2)}, u32[]{:S(2)}) collective-permute-start(f32[128,128]{1,0:T(8,128)S(1)} %add_add_fusion), channel_id=1, source_target_pairs={{0,16},{16,0},{1,17},{17,1},{2,18},{18,2},{3,19},{19,3},{4,20},{20... | collective-permute-start | bytes 196616 | tf_op jit(solution)/shard_map/ppermute | solution.py:30
  (61 shorter events, 13.2 us)
Async XLA Ops:
  7.2 93.5 %copy-start = (bf16[256,256]{1,0:T(8,128)(2,1)S(1)}, bf16[256,256]{1,0:T(8,128)(2,1)}, u32[]{:S(2)}) copy-start(bf16[256,256]{1,0:T(8,128)(2,1)} %param.5) | copy-start | bytes 393220
  9.8 13.0 %copy-start.2 = (bf16[256,256]{1,0:T(8,128)(2,1)S(1)}, bf16[256,256]{1,0:T(8,128)(2,1)}, u32[]{:S(2)}) copy-start(bf16[256,256]{1,0:T(8,128)(2,1)} %param.6) | copy-start | bytes 393220
  9.8 13.2 %copy-start.1 = (bf16[256,256]{1,0:T(8,128)(2,1)S(1)}, bf16[256,256]{1,0:T(8,128)(2,1)}, u32[]{:S(2)}) copy-start(bf16[256,256]{1,0:T(8,128)(2,1)} %param.7) | copy-start | bytes 393220
  9.8 99.5 %all-to-all-start = ((bf16[32,256,128]{2,1,0:T(8,128)(2,1)}), bf16[32,256,128]{2,1,0:T(8,128)(2,1)S(1)}, u32[]{:S(2)}, u32[]{:S(2)}) async-start(bf16[32,256,128]{2,1,0:T(8,128)(2,1)} %stack.17), calls=%async_computation | async-start | bytes 4194304 | tf_op jit(solution)/shard_map/all_to_all | solution.py:21
  22.1 92.7 %all-gather.2.cloned.1.call-start = ((), (), s32[]{:S(2)}) async-start(), calls=%async_computation.1 | async-start | bytes 2228224 | tf_op jit(solution)/shard_map/all_gather | solution.py:68
  23.2 3.2 %collective-permute-start = (f32[2,128,128]{2,1,0:T(8,128)S(1)}, f32[2,128,128]{2,1,0:T(8,128)S(1)}, u32[]{:S(2)}, u32[]{:S(2)}) collective-permute-start(f32[2,128,128]{2,1,0:T(8,128)S(1)} %fusion.11), channel_id=1, source_target_pairs={{0,16},{16,0},{1,17},{17,1},{2,18},{18,2},{3,19},{19,3},{4,20},{20... | collective-permute-start | bytes 393224 | tf_op jit(solution)/shard_map/ppermute | solution.py:30
  26.4 42.5 %collective-permute-start.1 = (f32[128,128]{1,0:T(8,128)S(1)}, f32[128,128]{1,0:T(8,128)S(1)}, u32[]{:S(2)}, u32[]{:S(2)}) collective-permute-start(f32[128,128]{1,0:T(8,128)S(1)} %add_bitcast_fusion.1), channel_id=1, source_target_pairs={{0,32},{32,64},{64,96},{96,128},{128,160},{160,192},{192,224},{224... | collective-permute-start | bytes 196616 | tf_op jit(solution)/shard_map/ppermute | solution.py:53
  69.0 7.3 %collective-permute-start.2 = (f32[128,128]{1,0:T(8,128)S(1)}, f32[128,128]{1,0:T(8,128)S(1)}, u32[]{:S(2)}, u32[]{:S(2)}) collective-permute-start(f32[128,128]{1,0:T(8,128)S(1)} %add.79), channel_id=1, source_target_pairs={{0,64},{32,96},{64,128},{96,160},{128,192},{160,224},{192,256},{22... | collective-permute-start | bytes 196616 | tf_op jit(solution)/shard_map/ppermute | solution.py:53
  76.3 10.3 %collective-permute-start.3 = (f32[128,128]{1,0:T(8,128)S(1)}, f32[128,128]{1,0:T(8,128)S(1)}, u32[]{:S(2)}, u32[]{:S(2)}) collective-permute-start(f32[128,128]{1,0:T(8,128)S(1)} %add.81), channel_id=1, source_target_pairs={{0,128},{32,160},{64,192},{96,224},{128,256},{160,288},{192,320},{... | collective-permute-start | bytes 196616 | tf_op jit(solution)/shard_map/ppermute | solution.py:53
  85.3 17.4 %copy-start.8 = (pred[256,256]{1,0:T(8,128)(4,1)}, pred[256,256]{1,0:T(8,128)(4,1)S(1)}, u32[]{:S(2)}) copy-start(pred[256,256]{1,0:T(8,128)(4,1)S(1)} %iota_compare_fusion) | copy-start | bytes 196612
  86.6 15.4 %collective-permute-start.4 = (f32[128,128]{1,0:T(8,128)S(1)}, f32[128,128]{1,0:T(8,128)S(1)}, u32[]{:S(2)}, u32[]{:S(2)}) collective-permute-start(f32[128,128]{1,0:T(8,128)S(1)} %add.83), channel_id=1, source_target_pairs={{0,256},{32,288},{64,320},{96,352},{128,384},{160,416},{192,448},{... | collective-permute-start | bytes 196616 | tf_op jit(solution)/shard_map/ppermute | solution.py:53
  102.7 4.7 %collective-permute-start.5 = (f32[128,128]{1,0:T(8,128)}, f32[128,128]{1,0:T(8,128)}, u32[]{:S(2)}, u32[]{:S(2)}) collective-permute-start(f32[128,128]{1,0:T(8,128)} %add_add_fusion.1), channel_id=1, source_target_pairs={{0,16},{16,0},{1,17},{17,1},{2,18},{18,2},{3,19},{19,3},{4,20},{20... | collective-permute-start | bytes 196616 | tf_op jit(solution)/shard_map/ppermute | solution.py:30
  108.2 1.1 copy-start.4
  108.2 1.1 copy-start.6
  112.0 2.9 %copy-start.3 = (f32[256,2,128]{0,2,1:T(8,128)S(1)}, f32[256,2,128]{0,2,1:T(8,128)}, u32[]{:S(2)}) copy-start(f32[256,2,128]{0,2,1:T(8,128)} %get-tuple-element.14) | copy-start | bytes 786436
  117.2 10.0 %copy-start.9 = (pred[256,256]{1,0:T(8,128)(4,1)S(1)}, pred[256,256]{1,0:T(8,128)(4,1)}, u32[]{:S(2)}) copy-start(pred[256,256]{1,0:T(8,128)(4,1)} %copy-done.8) | copy-start | bytes 196612
  117.5 3.2 %collective-permute-start.6 = (f32[2,128,128]{2,1,0:T(8,128)S(1)}, f32[2,128,128]{2,1,0:T(8,128)S(1)}, u32[]{:S(2)}, u32[]{:S(2)}) collective-permute-start(f32[2,128,128]{2,1,0:T(8,128)S(1)} %convolution_bitcast_fusion.6), channel_id=1, source_target_pairs={{0,16},{16,0},{1,17},{17,1},{2,18},{18,2},{3,19},{19,3},{4,20},{20... | collective-permute-start | bytes 393224 | tf_op jit(solution)/shard_map/ppermute | solution.py:30
  120.8 33.0 %copy-start.5 = (f32[1,128,128]{2,1,0:T(8,128)S(1)}, f32[1,128,128]{2,1,0:T(8,128)}, u32[]{:S(2)}) copy-start(f32[1,128,128]{2,1,0:T(8,128)} %copy-done.4) | copy-start | bytes 196612
  120.8 33.0 %copy-start.7 = (f32[1,128,128]{2,1,0:T(8,128)S(1)}, f32[1,128,128]{2,1,0:T(8,128)}, u32[]{:S(2)}) copy-start(f32[1,128,128]{2,1,0:T(8,128)} %copy-done.6) | copy-start | bytes 196612
  120.8 5.1 %collective-permute-start.7 = (f32[128,128]{1,0:T(8,128)S(1)}, f32[128,128]{1,0:T(8,128)S(1)}, u32[]{:S(2)}, u32[]{:S(2)}) collective-permute-start(f32[128,128]{1,0:T(8,128)S(1)} %add_bitcast_fusion), channel_id=1, source_target_pairs={{32,0},{64,32},{96,64},{128,96},{160,128},{192,160},{224,192},{256... | collective-permute-start | bytes 196616 | tf_op jit(solution)/shard_map/ppermute | solution.py:53
  126.0 6.6 %collective-permute-start.8 = (f32[128,128]{1,0:T(8,128)S(1)}, f32[128,128]{1,0:T(8,128)S(1)}, u32[]{:S(2)}, u32[]{:S(2)}) collective-permute-start(f32[128,128]{1,0:T(8,128)S(1)} %add.91), channel_id=1, source_target_pairs={{64,0},{96,32},{128,64},{160,96},{192,128},{224,160},{256,192},{28... | collective-permute-start | bytes 196616 | tf_op jit(solution)/shard_map/ppermute | solution.py:53
  132.6 8.9 %collective-permute-start.9 = (f32[128,128]{1,0:T(8,128)S(1)}, f32[128,128]{1,0:T(8,128)S(1)}, u32[]{:S(2)}, u32[]{:S(2)}) collective-permute-start(f32[128,128]{1,0:T(8,128)S(1)} %add.93), channel_id=1, source_target_pairs={{128,0},{160,32},{192,64},{224,96},{256,128},{288,160},{320,192},{... | collective-permute-start | bytes 196616 | tf_op jit(solution)/shard_map/ppermute | solution.py:53
  141.5 5.0 %collective-permute-start.10 = (f32[128,128]{1,0:T(8,128)S(1)}, f32[128,128]{1,0:T(8,128)S(1)}, u32[]{:S(2)}, u32[]{:S(2)}) collective-permute-start(f32[128,128]{1,0:T(8,128)S(1)} %add.95), channel_id=1, source_target_pairs={{256,0},{288,32},{320,64},{352,96},{384,128},{416,160},{448,192},{... | collective-permute-start | bytes 196616 | tf_op jit(solution)/shard_map/ppermute | solution.py:53
  146.6 8.3 %collective-permute-start.11 = (f32[128,128]{1,0:T(8,128)S(1)}, f32[128,128]{1,0:T(8,128)S(1)}, u32[]{:S(2)}, u32[]{:S(2)}) collective-permute-start(f32[128,128]{1,0:T(8,128)S(1)} %add_add_fusion), channel_id=1, source_target_pairs={{0,16},{16,0},{1,17},{17,1},{2,18},{18,2},{3,19},{19,3},{4,20},{20... | collective-permute-start | bytes 196616 | tf_op jit(solution)/shard_map/ppermute | solution.py:30
Sparse Core Ops, SparseCore 0:
  25.9 64.3 all-gather.1
